TPU v7x, 512 devices: a whole 4x4x16 slice. The times are simulated.
512 devices in a mesh: ctx: 64 (over x, z_lo, core), head: 8 (over y, z_hi).
Axes of the slice: x: 4, y: 4, z: 16 (z_hi: 2, z_lo: 8; z = z_hi * 8 + z_lo), core: 2. Of those that a mesh axis runs over, the one named last changes fastest.
Arguments:
- queries: bfloat16 [16384, 2048], P('ctx', 'head'), may hold values from -40 to 40
- keys: bfloat16 [16384, 2048], P('ctx', 'head'), may hold values from -4 to 4
- values: bfloat16 [16384, 2048], P('ctx', 'head'), may hold values from -5 to 5
- selected: int32 [16, 512, 3], P('head', 'ctx'), may hold values from 0 to 63, as said below
- out_weight: bfloat16 [2048, 2048], P(None, 'head'), may hold values from -0.125 to 0.125
Outputs:
- projected: bfloat16 [16384, 2048], P('ctx', 'head')
Inputs may be any that keep to these rules, and one draw needn't show every extreme that they name: `selected`: entry 0 of a tile's selection is its own block; entries 1 and 2 are two different earlier blocks, or both the own block where no earlier block is chosen for the tile (one earlier block and the own block in the second key block). For each head, the tiles of one key block name any one other block at most 2 times, and exactly 2 times for every block they name, from the third key block on.
All inputs are finite; a program needn't handle non-finite values.
Results may differ from a plain program's by a relative error of at most 0.0054.
Values may be sent and summed in bfloat16 or wider, within the bound.
No kernel may reach another device: no remote copies, remote signals or barrier semaphores. Data moves between devices by JAX's collectives and lax.ppermute only.
A program may use at most 64 MiB of HBM per device.

v0:
```python
import jax
import jax.numpy as jnp
from jax import lax
from jax.sharding import Mesh, PartitionSpec as P

CAP = 2
LANE_ROWS = 4
LSE_ROWS = 16


def split_bf16(x):
    hi = lax.reduce_precision(x, exponent_bits=8, mantissa_bits=7)
    rest = x - hi
    mid = lax.reduce_precision(rest, exponent_bits=8, mantissa_bits=7)
    lo = rest - mid
    return jnp.stack([hi, mid, lo]).astype(jnp.bfloat16)


def join_bf16(parts):
    parts = parts.astype(jnp.float32)
    return parts[0] + (parts[1] + parts[2])


def softmax_pv(scores, vals):
    top = jnp.max(scores, axis=-1)
    prob = jnp.exp(scores - top[..., None])
    total = jnp.sum(prob, axis=-1)
    part = jnp.einsum(
        "hrk,khd->hrd", prob.astype(jnp.bfloat16), vals, preferred_element_type=jnp.float32
    )
    return (part / total[..., None], top + jnp.log(total))


def local(queries, keys, values, selected, out_weight):
    heads_loc = selected.shape[0]
    tiles = selected.shape[1]
    tokens_here = queries.shape[0]
    width = queries.shape[1] // heads_loc
    tile_rows = tokens_here // tiles
    sources = lax.axis_size("ctx")
    mine = lax.axis_index("ctx")
    scale = width ** (-0.5)
    quer_three = queries.reshape(tokens_here, heads_loc, width)
    keys_three = keys.reshape(tokens_here, heads_loc, width)
    vals_three = values.reshape(tokens_here, heads_loc, width)
    pos = jnp.arange(tokens_here, dtype=jnp.int32)
    own_scores = (
        jnp.einsum("rhd,khd->hrk", quer_three, keys_three, preferred_element_type=jnp.float32)
        * scale
    )
    own_scores = jnp.where((pos[:, None] >= pos[None, :])[None], own_scores, jnp.float32(-1e30))
    own_out, own_lse = softmax_pv(own_scores, vals_three)
    own_out = own_out.reshape(heads_loc, tiles, tile_rows, width)
    own_lse = own_lse.reshape(heads_loc, tiles, tile_rows)
    picks = selected[:, :, 1:]
    valid = picks != mine
    target = jnp.where(valid, picks, sources)
    onehot = (target[..., None] == jnp.arange(sources, dtype=jnp.int32)).astype(jnp.int32)
    flat_hot = onehot.reshape(heads_loc, tiles * 2, sources)
    before = jnp.cumsum(flat_hot, axis=1) - flat_hot
    slot = jnp.sum(before * flat_hot, axis=-1).reshape(heads_loc, tiles, 2)
    query_src = jnp.transpose(
        quer_three.reshape(tiles, tile_rows, heads_loc, width), (2, 0, 1, 3)
    ).reshape(heads_loc, tiles, tile_rows * width)
    flat_slot = target * CAP + slot
    route = (flat_slot[..., None] == jnp.arange(sources * CAP, dtype=jnp.int32)).astype(
        jnp.bfloat16
    )
    send_q = jnp.einsum(
        "htep,htx->phx", route, query_src, preferred_element_type=jnp.float32
    ).astype(jnp.bfloat16)
    send_q = send_q.reshape(sources, CAP, heads_loc, tile_rows, width)
    got_rows = lax.all_to_all(send_q, "ctx", split_axis=0, concat_axis=0, tiled=True)
    got_q = jnp.transpose(got_rows, (2, 0, 1, 3, 4)).reshape(
        heads_loc, sources * CAP * tile_rows, width
    )
    got_scores = (
        jnp.einsum("hrd,khd->hrk", got_q, keys_three, preferred_element_type=jnp.float32) * scale
    )
    part, lse = softmax_pv(got_scores, vals_three)
    part = jnp.transpose(
        part.reshape(heads_loc, sources, CAP, tile_rows, width), (1, 2, 0, 3, 4)
    ).reshape(sources, CAP * heads_loc * tile_rows, width)
    pieces = split_bf16(lse.reshape(heads_loc, sources, CAP, tile_rows))
    pieces = jnp.concatenate(
        [pieces, jnp.zeros((LANE_ROWS - 3,) + pieces.shape[1:], pieces.dtype)], axis=0
    )
    lse_rows = jnp.transpose(pieces, (2, 3, 1, 0, 4)).reshape(
        sources, CAP * heads_loc, LANE_ROWS * tile_rows
    )
    rows_part = CAP * heads_loc * tile_rows
    pad = -(rows_part + CAP * heads_loc) % 16
    back = jnp.concatenate(
        [part.astype(jnp.bfloat16), lse_rows, jnp.zeros((sources, pad, width), jnp.bfloat16)],
        axis=1,
    )
    got_back = lax.all_to_all(back, "ctx", split_axis=0, concat_axis=0, tiled=True)
    got_out = got_back[:, :rows_part].reshape(sources * CAP, heads_loc, tile_rows, width)
    got_lse = got_back[:, rows_part : rows_part + CAP * heads_loc].reshape(
        sources * CAP, heads_loc, width
    )
    pick_out = jnp.einsum("htep,phrd->hterd", route, got_out, preferred_element_type=jnp.float32)
    pick_parts = jnp.einsum(
        "htep,phx->htex", route, got_lse, preferred_element_type=jnp.float32
    ).reshape(heads_loc, tiles, 2, LANE_ROWS, tile_rows)
    pick_lse = pick_parts[:, :, :, 0] + (pick_parts[:, :, :, 1] + pick_parts[:, :, :, 2])
    keep = valid[..., None]
    top = jnp.maximum(own_lse, jnp.max(jnp.where(keep, pick_lse, own_lse[:, :, None]), axis=2))
    own_w = jnp.exp(own_lse - top)
    pick_w = jnp.exp(jnp.where(keep, pick_lse - top[:, :, None], jnp.float32(-1e30)))
    numer = own_w[..., None] * own_out + jnp.sum(pick_w[..., None] * pick_out, axis=2)
    denom = own_w + jnp.sum(pick_w, axis=2)
    attention = jnp.transpose(numer / denom[..., None], (1, 2, 0, 3)).reshape(
        tokens_here, heads_loc * width
    )
    attention = attention.astype(jnp.bfloat16)
    pair = lax.axis_size("zh")
    mine_zh = lax.axis_index("zh")
    own_rows = lax.all_gather(attention, "y", axis=1, tiled=True)
    partner = lax.ppermute(attention, "zh", [(0, 1), (1, 0)])
    partner_rows = lax.all_gather(partner, "y", axis=1, tiled=True)
    groups = out_weight.reshape(-1, pair, heads_loc * width, out_weight.shape[1])
    own_w = lax.dynamic_index_in_dim(groups, mine_zh, axis=1, keepdims=False)
    partner_w = lax.dynamic_index_in_dim(groups, 1 - mine_zh, axis=1, keepdims=False)
    projected = jnp.dot(
        own_rows, own_w.reshape(-1, out_weight.shape[1]), preferred_element_type=jnp.float32
    ) + jnp.dot(
        partner_rows, partner_w.reshape(-1, out_weight.shape[1]), preferred_element_type=jnp.float32
    )
    return projected.astype(jnp.bfloat16)


def solution(mesh):
    ctx_n, head_n = mesh.devices.shape
    split = Mesh(mesh.devices.reshape(ctx_n, head_n // 2, 2), ("ctx", "y", "zh"))
    head = ("y", "zh")
    return jax.shard_map(
        local,
        mesh=split,
        in_specs=(
            P("ctx", head),
            P("ctx", head),
            P("ctx", head),
            P(head, "ctx", None),
            P(None, head),
        ),
        out_specs=P("ctx", head),
        check_vma=False,
    )
```

profile of v0, /device:TPU:2, one launch (start us, length us, event | category | flops | bytes accessed | tf_op | source)
XLA Modules:
  0.0 310.1 jit_solution(9879162235493104044)
XLA Ops:
  0.0 0.0 copy-start
  0.0 0.7 slice.18
  0.7 0.1 copy.102
  0.8 0.1 eq.29
  0.9 0.1 fusion.51
  1.0 0.2 select_reduce_fusion
  1.2 0.1 reshape.199
  1.3 0.1 copy.69
  1.4 0.6 copy-done.10
  2.0 0.1 convert_reduce_fusion
  2.0 0.9 reshape_reshape.3
  3.0 0.7 convolution_convert_fusion
  3.7 0.5 copy.109
  4.2 1.8 copy.71
  6.0 16.1 %all-to-all-start = ((bf16[64,2,2,32,128]{4,3,1,2,0:T(8,128)(2,1)}), bf16[64,2,2,32,128]{4,3,1,2,0:T(8,128)(2,1)S(1)}, u32[]{:S(2)}, u32[]{:S(2)}) async-start(bf16[64,2,2,32,128]{4,3,1,2,0:T(8,128)(2,1)} %copy.71), calls=%async_computation | async-start | bytes 4194304 | tf_op jit(solution)/shard_map/all_to_all | solution.py:73
  22.1 0.1 pad.3.clone
  22.2 94.5 %all-to-all-done = bf16[64,2,2,32,128]{4,3,1,2,0:T(8,128)(2,1)S(1)} async-done(((bf16[64,2,2,32,128]{4,3,1,2,0:T(8,128)(2,1)}), bf16[64,2,2,32,128]{4,3,1,2,0:T(8,128)(2,1)S(1)}, u32[]{:S(2)}, u32[]{:S(2)}) %all-to-all-start) | async-done | bytes 2097184 | tf_op jit(solution)/shard_map/all_to_all | solution.py:73
  116.7 0.5 copy.72
  117.2 0.0 copy-done
  117.2 1.3 multiply_reduce_fusion
  118.5 0.0 copy-start.1
  118.5 0.0 copy-start.12
  118.5 1.4 fusion
  119.9 1.8 copy-done.1
  121.7 0.2 add.91
  121.9 0.1 copy.77
  122.1 0.1 copy.80
  122.2 0.0 copy-done.12
  122.2 5.0 %fusion.2 = bf16[2,4096,128]{2,1,0:T(8,128)(2,1)S(1)} fusion(f32[2,4096,256]{1,2,0:T(8,128)} %copy-done.1, f32[2,4096]{1,0:T(2,128)S(1)} %get-tuple-element.17, f32[2,4096]{1,0:T(2,128)S(1)} %fusion, bf16[256,256]{1,0:T(8,128)(2,1)S(1)} %copy-done.12), kind=kOutput, calls=%fused_computation.6 | convolution fusion | flops 545259520 | bytes 10682368 | tf_op jit(solution)/shard_map/hrk,khd->hrd/dot_general | solution.py:28
  127.2 0.6 copy.76
  127.8 0.0 copy-start.6
  127.8 1.9 maximum_maximum_fusion
  129.7 9.8 %all-to-all-start.1 = ((bf16[64,144,128]{2,1,0:T(8,128)(2,1)}), bf16[64,144,128]{2,1,0:T(8,128)(2,1)S(1)}, u32[]{:S(2)}, u32[]{:S(2)}) async-start(bf16[64,144,128]{2,1,0:T(8,128)(2,1)} %maximum_maximum_fusion), calls=%async_computation.1 | async-start | bytes 4718592 | tf_op jit(solution)/shard_map/all_to_all | solution.py:97
  139.6 0.2 fusion.60
  139.9 0.8 copy-done.2
  140.7 0.1 fusion.17
  140.7 0.0 copy-start.9
  140.8 0.1 add.88
  140.9 0.1 copy.68
  141.0 0.4 copy-done.9
  141.3 1.3 constant_dynamic-slice_fusion.1
  142.6 2.1 convolution_divide_fusion.1
  144.7 100.3 %all-to-all-done.1 = bf16[64,144,128]{2,1,0:T(8,128)(2,1)S(1)} async-done(((bf16[64,144,128]{2,1,0:T(8,128)(2,1)}), bf16[64,144,128]{2,1,0:T(8,128)(2,1)S(1)}, u32[]{:S(2)}, u32[]{:S(2)}) %all-to-all-start.1) | async-done | bytes 2359328 | tf_op jit(solution)/shard_map/all_to_all | solution.py:97
  245.1 1.4 fusion.44
  246.6 1.4 reshape.206
  248.0 1.0 fusion.59
  249.0 0.1 fusion.46
  249.1 1.9 fusion.57
  251.0 1.4 copy.89
  252.5 1.3 fusion.56
  253.8 1.4 copy.85
  255.1 1.4 copy.91
  256.5 0.3 slice.28
  256.8 0.5 copy-done.7
  257.4 1.2 fusion.12
  258.6 0.0 copy-done.3
  258.6 0.2 fusion.38
  258.9 0.1 copy.92
  259.1 14.0 %all_gather.6 = bf16[256,1024]{1,0:T(8,128)(2,1)S(1)} all-gather(bf16[256,256]{1,0:T(8,128)(2,1)S(1)} %bitcast.112), channel_id=1, replica_groups=mesh['ctx'=64,'y'=4,'zh'=2] {'y'}, dimensions={1}, use_global_device_ids=true | all-gather | bytes 655360 | tf_op jit(solution)/shard_map/all_gather | solution.py:119
  273.1 8.2 %collective-permute-start = (bf16[256,256]{1,0:T(8,128)(2,1)S(1)}, bf16[256,256]{1,0:T(8,128)(2,1)S(1)}, u32[]{:S(2)}, u32[]{:S(2)}) collective-permute-start(bf16[256,256]{1,0:T(8,128)(2,1)S(1)} %bitcast.113), channel_id=1, source_target_pairs={{0,1},{1,0},{2,3},{3,2},{4,5},{5,4},{6,7},{7,6},{8,9},{9,8},{10,11... | collective-permute-start | bytes 393224 | tf_op jit(solution)/shard_map/ppermute | solution.py:120
  281.3 0.3 fusion.61
  281.6 14.2 %collective-permute-done = bf16[256,256]{1,0:T(8,128)(2,1)S(1)} collective-permute-done((bf16[256,256]{1,0:T(8,128)(2,1)S(1)}, bf16[256,256]{1,0:T(8,128)(2,1)S(1)}, u32[]{:S(2)}, u32[]{:S(2)}) %collective-permute-start) | collective-permute-done | bytes 131104 | tf_op jit(solution)/shard_map/ppermute | solution.py:120
  295.8 13.3 %all_gather.7 = bf16[256,1024]{1,0:T(8,128)(2,1)S(1)} all-gather(bf16[256,256]{1,0:T(8,128)(2,1)S(1)} %collective-permute-done), channel_id=1, replica_groups=mesh['ctx'=64,'y'=4,'zh'=2] {'y'}, dimensions={1}, use_global_device_ids=true | all-gather | bytes 655360 | tf_op jit(solution)/shard_map/all_gather | solution.py:121
  309.1 1.0 fusion.15
  (27 shorter events, 0.3 us)
Async XLA Ops:
  0.0 117.2 %copy-start = (bf16[256,256]{1,0:T(8,128)(2,1)S(1)}, bf16[256,256]{1,0:T(8,128)(2,1)}, u32[]{:S(2)}) copy-start(bf16[256,256]{1,0:T(8,128)(2,1)} %param.6) | copy-start | bytes 393220
  1.4 0.6 copy-start.10
  6.0 110.7 %all-to-all-start = ((bf16[64,2,2,32,128]{4,3,1,2,0:T(8,128)(2,1)}), bf16[64,2,2,32,128]{4,3,1,2,0:T(8,128)(2,1)S(1)}, u32[]{:S(2)}, u32[]{:S(2)}) async-start(bf16[64,2,2,32,128]{4,3,1,2,0:T(8,128)(2,1)} %copy.71), calls=%async_computation | async-start | bytes 4194304 | tf_op jit(solution)/shard_map/all_to_all | solution.py:73
  118.5 3.2 %copy-start.1 = (f32[2,4096,256]{1,2,0:T(8,128)}, f32[2,4096,256]{1,2,0:T(8,128)S(1)}, u32[]{:S(2)}) copy-start(f32[2,4096,256]{1,2,0:T(8,128)S(1)} %get-tuple-element.18) | copy-start | bytes 25165828
  118.5 3.7 %copy-start.12 = (bf16[256,256]{1,0:T(8,128)(2,1)S(1)}, bf16[256,256]{1,0:T(8,128)(2,1)}, u32[]{:S(2)}) copy-start(bf16[256,256]{1,0:T(8,128)(2,1)} %param.7) | copy-start | bytes 393220
  127.8 11.8 %copy-start.6 = (bf16[256,256]{1,0:T(8,128)(2,1)S(1)}, bf16[256,256]{1,0:T(8,128)(2,1)}, u32[]{:S(2)}) copy-start(bf16[256,256]{1,0:T(8,128)(2,1)} %param.5) | copy-start | bytes 393220
  129.7 115.3 %all-to-all-start.1 = ((bf16[64,144,128]{2,1,0:T(8,128)(2,1)}), bf16[64,144,128]{2,1,0:T(8,128)(2,1)S(1)}, u32[]{:S(2)}, u32[]{:S(2)}) async-start(bf16[64,144,128]{2,1,0:T(8,128)(2,1)} %maximum_maximum_fusion), calls=%async_computation.1 | async-start | bytes 4718592 | tf_op jit(solution)/shard_map/all_to_all | solution.py:97
  139.8 0.8 copy-start.2
  140.7 0.6 copy-start.9
  141.0 108.0 %copy-start.8 = (pred[2,8,2]{1,2,0:T(4,128)(4,1)}, pred[2,8,2]{1,2,0:T(4,128)(4,1)S(1)}, u32[]{:S(2)}) copy-start(pred[2,8,2]{1,2,0:T(4,128)(4,1)S(1)} %copy.68) | copy-start | bytes 100
  253.8 3.1 copy-start.11
  256.5 0.8 copy-start.7
  256.5 2.1 copy-start.3
  256.5 2.1 copy-start.4
  256.5 2.1 copy-start.5
  273.1 22.7 %collective-permute-start = (bf16[256,256]{1,0:T(8,128)(2,1)S(1)}, bf16[256,256]{1,0:T(8,128)(2,1)S(1)}, u32[]{:S(2)}, u32[]{:S(2)}) collective-permute-start(bf16[256,256]{1,0:T(8,128)(2,1)S(1)} %bitcast.113), channel_id=1, source_target_pairs={{0,1},{1,0},{2,3},{3,2},{4,5},{5,4},{6,7},{7,6},{8,9},{9,8},{10,11... | collective-permute-start | bytes 393224 | tf_op jit(solution)/shard_map/ppermute | solution.py:120
where the time goes:
time: 311 us; the launch traced here: 310 us
  waiting for transfers between devices  209 us (67%)
  starting transfers between devices  34.1 us (11%)
  blocking collectives  27.3 us (9%)
  local copies, waits for them, and re-layouts  18.4 us (6%)
  matrix products  13.4 us (4%)
  other arithmetic  7.55 us (2%)
    all_to_all x1, waiting for transfers between devices, local(): lax.all_to_all(back, 'ctx', split_axis=0, concat_axis=0, tiled=True)  100 us
    all_to_all x1, waiting for transfers between devices, local(): lax.all_to_all(send_q, 'ctx', split_axis=0, concat_axis=0, tiled=True)  94.5 us
    all_to_all x1, starting transfers between devices, local(): lax.all_to_all(send_q, 'ctx', split_axis=0, concat_axis=0, tiled=True)  16.1 us
    ppermute x1, waiting for transfers between devices, local(): partner = lax.ppermute(attention, 'zh', [(0, 1), (1, 0)])  14.2 us
    all_gather x1, blocking collectives, local(): own_rows = lax.all_gather(attention, 'y', axis=1, tiled=True)  14 us
    all_gather x1, blocking collectives, local(): partner_rows = lax.all_gather(partner, 'y', axis=1, tiled=True)  13.3 us
    all_to_all x1, starting transfers between devices, local(): lax.all_to_all(back, 'ctx', split_axis=0, concat_axis=0, tiled=True)  9.81 us
    ppermute x1, starting transfers between devices, local(): partner = lax.ppermute(attention, 'zh', [(0, 1), (1, 0)])  8.2 us
  transfers between devices with their start and end apart: 3, of which 3 were waited for; matrix products, arithmetic and copies ran while one was open for 1% of the time, Pallas kernels for 0%

commit v1 on v0

--- a/solution.py
+++ b/solution.py
@@ -116,7 +116,9 @@
     attention = attention.astype(jnp.bfloat16)
     pair = lax.axis_size("zh")
     mine_zh = lax.axis_index("zh")
-    own_rows = lax.all_gather(attention, "y", axis=1, tiled=True)
+    own_rows = jnp.concatenate(
+        lax.all_to_all(jnp.stack([attention] * lax.axis_size("y")), "y", 0, 0), axis=1
+    )
     partner = lax.ppermute(attention, "zh", [(0, 1), (1, 0)])
     partner_rows = lax.all_gather(partner, "y", axis=1, tiled=True)
     groups = out_weight.reshape(-1, pair, heads_loc * width, out_weight.shape[1])

time: 311 us -> 296 us (0.952)
  the two profiles are of different devices: /device:TPU:2 before, /device:TPU:14 now
where the time goes in v1:
time: 296 us
  waiting for transfers between devices  215 us (73%)
  starting transfers between devices  39.1 us (13%)
  blocking collectives  13.4 us (5%)
  local copies, waits for them, and re-layouts  12 us (4%)
  matrix products  11 us (4%)
  other arithmetic  4.41 us (1%)
    all_to_all x1, waiting for transfers between devices, local(): lax.all_to_all(back, 'ctx', split_axis=0, concat_axis=0, tiled=True)  104 us
    all_to_all x1, waiting for transfers between devices, local(): lax.all_to_all(send_q, 'ctx', split_axis=0, concat_axis=0, tiled=True)  94.5 us
    ppermute x1, waiting for transfers between devices, local(): partner = lax.ppermute(attention, 'zh', [(0, 1), (1, 0)])  17 us
    all_to_all x1, starting transfers between devices, local(): lax.all_to_all(send_q, 'ctx', split_axis=0, concat_axis=0, tiled=True)  16.2 us
    all_gather x1, blocking collectives, local(): partner_rows = lax.all_gather(partner, 'y', axis=1, tiled=True)  13.4 us
    all_to_all x1, starting transfers between devices, local(): lax.all_to_all(back, 'ctx', split_axis=0, concat_axis=0, tiled=True)  9.79 us
    ppermute x1, starting transfers between devices, local(): partner = lax.ppermute(attention, 'zh', [(0, 1), (1, 0)])  8.21 us
    dot_general x2, matrix products, softmax_pv(): jnp.einsum('hrk,khd->hrd', prob.astype(jnp.bfloat16), vals, preferred_ele...  6.02 us
  transfers between devices with their start and end apart: 4, of which 3 were waited for; matrix products, arithmetic and copies ran while one was open for 1% of the time, Pallas kernels for 0%

profile of v1, /device:TPU:14, one launch (start us, length us, event | category | flops | bytes accessed | tf_op | source)
XLA Modules:
  0.0 295.8 jit_solution(5433428052232075533)
XLA Ops:
  0.0 0.0 copy-start
  0.0 0.7 slice.18
  0.7 0.1 copy.105
  0.8 0.1 eq.29
  0.9 0.1 fusion.51
  1.0 0.2 select_reduce_fusion
  1.2 0.1 reshape.208
  1.3 0.1 copy.71
  1.4 0.1 convert_reduce_fusion
  1.5 1.0 reshape_reshape.3
  2.4 0.7 convolution_convert_fusion
  3.2 0.5 copy.112
  3.6 1.8 copy.73
  5.5 16.2 %all-to-all-start = ((bf16[64,2,2,32,128]{4,3,1,2,0:T(8,128)(2,1)}), bf16[64,2,2,32,128]{4,3,1,2,0:T(8,128)(2,1)S(1)}, u32[]{:S(2)}, u32[]{:S(2)}) async-start(bf16[64,2,2,32,128]{4,3,1,2,0:T(8,128)(2,1)} %copy.73), calls=%async_computation | async-start | bytes 4194304 | tf_op jit(solution)/shard_map/all_to_all | solution.py:73
  21.7 0.1 pad.3.clone
  21.8 94.5 %all-to-all-done = bf16[64,2,2,32,128]{4,3,1,2,0:T(8,128)(2,1)S(1)} async-done(((bf16[64,2,2,32,128]{4,3,1,2,0:T(8,128)(2,1)}), bf16[64,2,2,32,128]{4,3,1,2,0:T(8,128)(2,1)S(1)}, u32[]{:S(2)}, u32[]{:S(2)}) %all-to-all-start) | async-done | bytes 2097184 | tf_op jit(solution)/shard_map/all_to_all | solution.py:73
  116.3 0.5 copy.74
  116.8 0.0 copy-done
  116.8 1.3 multiply_reduce_fusion
  118.1 0.0 copy-start.1
  118.1 0.0 copy-start.8
  118.1 1.4 fusion
  119.5 1.8 copy-done.1
  121.3 0.2 add.91
  121.5 0.1 copy.79
  121.7 0.1 copy.82
  121.8 0.0 copy-done.8
  121.8 5.0 %fusion.2 = bf16[2,4096,128]{2,1,0:T(8,128)(2,1)S(1)} fusion(f32[2,4096,256]{1,2,0:T(8,128)} %copy-done.1, f32[2,4096]{1,0:T(2,128)S(1)} %get-tuple-element.17, f32[2,4096]{1,0:T(2,128)S(1)} %fusion, bf16[256,256]{1,0:T(8,128)(2,1)S(1)} %copy-done.8), kind=kOutput, calls=%fused_computation.6 | convolution fusion | flops 545259520 | bytes 10682368 | tf_op jit(solution)/shard_map/hrk,khd->hrd/dot_general | solution.py:28
  126.8 0.6 copy.78
  127.4 0.0 copy-start.6
  127.4 1.9 maximum_maximum_fusion
  129.3 9.8 %all-to-all-start.1 = ((bf16[64,144,128]{2,1,0:T(8,128)(2,1)}), bf16[64,144,128]{2,1,0:T(8,128)(2,1)S(1)}, u32[]{:S(2)}, u32[]{:S(2)}) async-start(bf16[64,144,128]{2,1,0:T(8,128)(2,1)} %maximum_maximum_fusion), calls=%async_computation.1 | async-start | bytes 4718592 | tf_op jit(solution)/shard_map/all_to_all | solution.py:97
  139.2 0.0 copy-done.6
  139.2 0.2 fusion.60
  139.4 0.1 fusion.17
  139.5 0.1 add.88
  139.6 0.1 copy.70
  139.7 1.0 convolution_divide_fusion.1
  140.7 103.9 %all-to-all-done.1 = bf16[64,144,128]{2,1,0:T(8,128)(2,1)S(1)} async-done(((bf16[64,144,128]{2,1,0:T(8,128)(2,1)}), bf16[64,144,128]{2,1,0:T(8,128)(2,1)S(1)}, u32[]{:S(2)}, u32[]{:S(2)}) %all-to-all-start.1) | async-done | bytes 2359328 | tf_op jit(solution)/shard_map/all_to_all | solution.py:97
  244.7 0.2 fusion.44
  244.9 0.1 reshape.215
  245.0 0.1 fusion.46
  245.1 0.1 fusion.57
  245.2 0.7 copy.91
  245.9 0.7 copy.87
  246.6 0.7 copy.93
  247.3 0.0 copy-start.2
  247.3 0.3 slice.28
  247.6 0.5 copy-done.7
  248.1 1.2 fusion.12
  249.4 0.0 copy-done.3
  249.4 0.0 copy-done.4
  249.4 0.2 fusion.38
  249.7 0.1 copy.94
  249.8 0.1 copy.95
  249.9 0.8 stack.6
  250.8 4.9 %all-to-all-start.2 = ((bf16[4,256,256]{1,2,0:T(8,128)(2,1)}), bf16[4,256,256]{1,2,0:T(8,128)(2,1)S(1)}, u32[]{:S(2)}, u32[]{:S(2)}) async-start(bf16[4,256,256]{1,2,0:T(8,128)(2,1)} %stack.6), calls=%async_computation.2 | async-start | bytes 1048576 | tf_op jit(solution)/shard_map/all_to_all | solution.py:120
  255.7 8.2 %collective-permute-start = (bf16[256,256]{1,0:T(8,128)(2,1)S(1)}, bf16[256,256]{1,0:T(8,128)(2,1)S(1)}, u32[]{:S(2)}, u32[]{:S(2)}) collective-permute-start(bf16[256,256]{1,0:T(8,128)(2,1)S(1)} %bitcast.118), channel_id=1, source_target_pairs={{0,1},{1,0},{2,3},{3,2},{4,5},{5,4},{6,7},{7,6},{8,9},{9,8},{10,11... | collective-permute-start | bytes 393224 | tf_op jit(solution)/shard_map/ppermute | solution.py:122
  263.9 0.1 constant_dynamic-slice_fusion.1
  264.0 17.0 %collective-permute-done = bf16[256,256]{1,0:T(8,128)(2,1)S(1)} collective-permute-done((bf16[256,256]{1,0:T(8,128)(2,1)S(1)}, bf16[256,256]{1,0:T(8,128)(2,1)S(1)}, u32[]{:S(2)}, u32[]{:S(2)}) %collective-permute-start) | collective-permute-done | bytes 131104 | tf_op jit(solution)/shard_map/ppermute | solution.py:122
  281.0 13.4 %all_gather.3 = bf16[256,1024]{1,0:T(8,128)(2,1)S(1)} all-gather(bf16[256,256]{1,0:T(8,128)(2,1)S(1)} %collective-permute-done), channel_id=1, replica_groups=mesh['ctx'=64,'y'=4,'zh'=2] {'y'}, dimensions={1}, use_global_device_ids=true | all-gather | bytes 655360 | tf_op jit(solution)/shard_map/all_gather | solution.py:123
  294.4 0.0 all-to-all-done.2
  294.4 0.3 fusion.61
  294.8 1.0 fusion.15
  (22 shorter events, 0.3 us)
Async XLA Ops:
  0.0 116.8 %copy-start = (bf16[256,256]{1,0:T(8,128)(2,1)S(1)}, bf16[256,256]{1,0:T(8,128)(2,1)}, u32[]{:S(2)}) copy-start(bf16[256,256]{1,0:T(8,128)(2,1)} %param.6) | copy-start | bytes 393220
  5.5 110.8 %all-to-all-start = ((bf16[64,2,2,32,128]{4,3,1,2,0:T(8,128)(2,1)}), bf16[64,2,2,32,128]{4,3,1,2,0:T(8,128)(2,1)S(1)}, u32[]{:S(2)}, u32[]{:S(2)}) async-start(bf16[64,2,2,32,128]{4,3,1,2,0:T(8,128)(2,1)} %copy.73), calls=%async_computation | async-start | bytes 4194304 | tf_op jit(solution)/shard_map/all_to_all | solution.py:73
  118.1 3.2 %copy-start.1 = (f32[2,4096,256]{1,2,0:T(8,128)}, f32[2,4096,256]{1,2,0:T(8,128)S(1)}, u32[]{:S(2)}) copy-start(f32[2,4096,256]{1,2,0:T(8,128)S(1)} %get-tuple-element.18) | copy-start | bytes 25165828
  118.1 3.7 %copy-start.8 = (bf16[256,256]{1,0:T(8,128)(2,1)S(1)}, bf16[256,256]{1,0:T(8,128)(2,1)}, u32[]{:S(2)}) copy-start(bf16[256,256]{1,0:T(8,128)(2,1)} %param.7) | copy-start | bytes 393220
  127.4 11.8 %copy-start.6 = (bf16[256,256]{1,0:T(8,128)(2,1)S(1)}, bf16[256,256]{1,0:T(8,128)(2,1)}, u32[]{:S(2)}) copy-start(bf16[256,256]{1,0:T(8,128)(2,1)} %param.5) | copy-start | bytes 393220
  129.3 115.3 %all-to-all-start.1 = ((bf16[64,144,128]{2,1,0:T(8,128)(2,1)}), bf16[64,144,128]{2,1,0:T(8,128)(2,1)S(1)}, u32[]{:S(2)}, u32[]{:S(2)}) async-start(bf16[64,144,128]{2,1,0:T(8,128)(2,1)} %maximum_maximum_fusion), calls=%async_computation.1 | async-start | bytes 4718592 | tf_op jit(solution)/shard_map/all_to_all | solution.py:97
  247.3 0.8 copy-start.7
  247.3 2.1 copy-start.3
  247.3 2.1 copy-start.4
  247.3 2.1 copy-start.5
  247.3 16.6 %copy-start.2 = (bf16[2048,256]{1,0:T(8,128)(2,1)S(1)}, bf16[2048,256]{1,0:T(8,128)(2,1)}, u32[]{:S(2)}) copy-start(bf16[2048,256]{1,0:T(8,128)(2,1)} %param.9) | copy-start | bytes 3145732
  250.8 43.7 %all-to-all-start.2 = ((bf16[4,256,256]{1,2,0:T(8,128)(2,1)}), bf16[4,256,256]{1,2,0:T(8,128)(2,1)S(1)}, u32[]{:S(2)}, u32[]{:S(2)}) async-start(bf16[4,256,256]{1,2,0:T(8,128)(2,1)} %stack.6), calls=%async_computation.2 | async-start | bytes 1048576 | tf_op jit(solution)/shard_map/all_to_all | solution.py:120
  255.7 25.3 %collective-permute-start = (bf16[256,256]{1,0:T(8,128)(2,1)S(1)}, bf16[256,256]{1,0:T(8,128)(2,1)S(1)}, u32[]{:S(2)}, u32[]{:S(2)}) collective-permute-start(bf16[256,256]{1,0:T(8,128)(2,1)S(1)} %bitcast.118), channel_id=1, source_target_pairs={{0,1},{1,0},{2,3},{3,2},{4,5},{5,4},{6,7},{7,6},{8,9},{9,8},{10,11... | collective-permute-start | bytes 393224 | tf_op jit(solution)/shard_map/ppermute | solution.py:122
